TPU v7x, 32 devices: a whole 2x2x4 slice. The times are simulated.
32 devices in a mesh: dp: 2 (over core), ctx: 4 (over z), expert: 4 (over y, x).
Axes of the slice: x: 2, y: 2, z: 4, core: 2. Of those that a mesh axis runs over, the one named last changes fastest.
Arguments:
- x_in: bfloat16 [4, 64, 8192], P('dp', 'ctx', 'expert'), may hold values from -6 to 6
- z_in: bfloat16 [4, 64, 8192], P('dp', 'ctx', 'expert'), may hold values from -6 to 6
- b_in: bfloat16 [4, 64, 128], P('dp', 'ctx'), may hold values from -0.5 to 0.5
- c_in: bfloat16 [4, 64, 128], P('dp', 'ctx'), may hold values from -0.75 to 0.75
- decay_log: float32 [4, 64, 128], P('dp', 'ctx', 'expert'), may hold values from -2 to 0, as said below
- skip: float32 [128], P('expert'), may hold values from 0.5 to 1.5
- out_weight: bfloat16 [8192, 4096], P('expert', 'ctx'), may hold values from -1 to 1
- moe_gain: float32 [4096], replicated, may hold values from 0.5 to 1.5
- gate_up: bfloat16 [4, 2, 7168, 4096], P('expert', None, ('dp', 'ctx')), may hold values from -0.09375 to 0.09375
- expert_ids: int32 [4, 64, 2], P('dp', ('ctx', 'expert')), may hold values from 0 to 3, as said below
- slot_ids: int32 [4, 64, 2], P('dp', ('ctx', 'expert')), may hold values from 0 to 7, as said below
Outputs:
- mamba_out: bfloat16 [4, 64, 4096], P('dp', ('ctx', 'expert'))
- expert_hidden: bfloat16 [4, 7168, 256], P('expert', ('dp', 'ctx'))
Inputs may be any that keep to these rules, and one draw needn't show every extreme that they name: `decay_log`: its values are negative. `expert_ids`: each token names two different experts. In the rows of one device (streams s with the same s // 2, positions t with the same t // 4) one expert, the same for all devices, is named by exactly 8 rows, and no expert by more than 8 rows. `slot_ids`: in the rows of one device the pairs (expert, slot) are all different.
All inputs are finite; a program needn't handle non-finite values.
Results may differ from a plain program's by a relative error of at most 0.0085.
Values may be sent and summed in bfloat16 or wider, within the bound.
No kernel may reach another device: no remote copies, remote signals or barrier semaphores. Data moves between devices by JAX's collectives and lax.ppermute only.
A program may use at most 128 MiB of HBM per device.

v0:
```python
import jax
import jax.numpy as jnp
from jax import lax
from jax.sharding import PartitionSpec as P

P_SIZE = 64
ALL_AXES = ("dp", "ctx", "expert")


def mixer(x_in, b_in, c_in, decay_log, skip):
    highest = lax.Precision.HIGHEST
    seq_count, total_len, width_in = x_in.shape
    head_count = skip.shape[0]
    state_size = b_in.shape[2]
    chunk = total_len if total_len <= 128 else 64
    chunks = total_len // chunk
    x_float = x_in.astype(jnp.float32).reshape(seq_count, chunks, chunk, head_count, P_SIZE)
    b_float = b_in.astype(jnp.float32).reshape(seq_count, chunks, chunk, state_size)
    c_float = c_in.astype(jnp.float32).reshape(seq_count, chunks, chunk, state_size)
    cum_decay = jnp.cumsum(decay_log.reshape(seq_count, chunks, chunk, head_count), axis=2)
    scores = jnp.einsum("sktn,skun->sktu", c_float, b_float, precision=highest)
    causal = (jnp.arange(chunk)[:, None] >= jnp.arange(chunk)[None, :])[None, None, :, :, None]
    spans = cum_decay[:, :, :, None, :] - cum_decay[:, :, None, :, :]
    kernel = jnp.where(causal, jnp.exp(jnp.where(causal, spans, 0.0)), 0.0) * scores[..., None]
    ssd = jnp.einsum("sktuh,skuhp->skthp", kernel, x_float, precision=highest)
    if chunks > 1:
        final_decay = cum_decay[:, :, -1, :]
        tails = jnp.exp(final_decay[:, :, None, :] - cum_decay)
        states = jnp.einsum("skuh,skuhp,skun->skhpn", tails, x_float, b_float, precision=highest)

        def step(carry, inputs):
            decay_k, state_k = inputs
            return (decay_k[:, :, None, None] * carry + state_k, carry)

        _, incoming = lax.scan(
            step,
            jnp.zeros_like(states[:, 0]),
            (jnp.moveaxis(jnp.exp(final_decay), 1, 0), jnp.moveaxis(states, 1, 0)),
        )
        incoming = jnp.moveaxis(incoming, 0, 1)
        ssd = ssd + jnp.exp(cum_decay)[..., None] * jnp.einsum(
            "sktn,skhpn->skthp", c_float, incoming, precision=highest
        )
    ssd = ssd + skip[None, None, None, :, None] * x_float
    return ssd.reshape(seq_count, total_len, width_in)


def expert_ffn(gate_up, slot_rows):
    both = jnp.einsum("gfd,qd->gfq", gate_up[0], slot_rows, preferred_element_type=jnp.float32)
    return (jax.nn.silu(both[0]) * both[1]).astype(jnp.bfloat16)


def dispatch_routed(partial_value, moe_gain, gate_up, expert_ids, slot_ids, capacity):
    seq_count = partial_value.shape[0]
    model_width = moe_gain.shape[0]
    per_block = expert_ids.shape[1]
    pick_count = expert_ids.shape[2]
    row_count = seq_count * per_block
    ctx_count = lax.axis_size("ctx")
    group_count = lax.axis_size("expert")
    grouped = partial_value.reshape(
        seq_count, ctx_count, group_count, per_block, partial_value.shape[2]
    )
    reduced = lax.psum_scatter(grouped, "expert", scatter_dimension=2, tiled=True).astype(
        jnp.bfloat16
    )
    swapped = lax.all_to_all(reduced, "ctx", split_axis=1, concat_axis=4, tiled=True)
    mamba_out = swapped.reshape(seq_count, per_block, model_width)
    flat = mamba_out.reshape(row_count, model_width).astype(jnp.float32)
    scale = lax.rsqrt(jnp.mean(flat * flat, axis=1, keepdims=True) + 1e-05)
    normed = (flat * scale * moe_gain[None, :]).astype(jnp.bfloat16)
    chosen = expert_ids.reshape(row_count, pick_count)
    placed = slot_ids.reshape(row_count, pick_count)
    match_expert = chosen[:, :, None, None] == jnp.arange(group_count)[None, None, :, None]
    match_slot = placed[:, :, None, None] == jnp.arange(capacity)[None, None, None, :]
    selector = (match_expert & match_slot).astype(jnp.bfloat16)
    outgoing = jnp.einsum(
        "rkec,rd->ecd", selector, normed, preferred_element_type=jnp.float32
    ).astype(jnp.bfloat16)
    arrived = lax.all_to_all(outgoing, "expert", split_axis=0, concat_axis=0, tiled=True)
    piece = lax.all_gather(arrived[None], ("dp", "ctx"), axis=0, tiled=True)
    slot_rows = piece.reshape(-1, piece.shape[3])
    return (mamba_out, expert_ffn(gate_up, slot_rows)[None])


def local(
    x_in, z_in, b_in, c_in, decay_log, skip, out_weight, moe_gain, gate_up, expert_ids, slot_ids
):
    seq_count, block_len, width_in = x_in.shape
    state_size = b_in.shape[2]
    model_width = moe_gain.shape[0]
    col_width = out_weight.shape[1]
    per_block = expert_ids.shape[1]
    pick_count = expert_ids.shape[2]
    dp_count = lax.axis_size("dp")
    ctx_count = lax.axis_size("ctx")
    group_count = lax.axis_size("expert")
    device_count = dp_count * ctx_count * group_count
    row_count = seq_count * per_block
    capacity = max(2, 4 * row_count // group_count)
    packed = jnp.concatenate([x_in, z_in, b_in, c_in], axis=2)
    packed = lax.all_gather(packed, "ctx", axis=1, tiled=True)
    decay_all = lax.all_gather(decay_log, "ctx", axis=1, tiled=True)
    route = jnp.stack([expert_ids, slot_ids], axis=-1)
    routes = lax.all_gather(route[None], ALL_AXES, axis=0, tiled=True)
    packed, decay_all, routes = lax.optimization_barrier((packed, decay_all, routes))
    x_all = packed[:, :, :width_in]
    z_all = packed[:, :, width_in : 2 * width_in]
    b_all = packed[:, :, 2 * width_in : 2 * width_in + state_size]
    c_all = packed[:, :, 2 * width_in + state_size :]
    ssd = mixer(x_all, b_all, c_all, decay_all, skip)
    gated = (ssd * jax.nn.silu(z_all.astype(jnp.float32))).astype(jnp.bfloat16)
    partial_value = jnp.einsum("stk,kd->std", gated, out_weight, preferred_element_type=jnp.float32)
    if device_count * row_count * model_width * 2 > 8 << 20:
        return dispatch_routed(partial_value, moe_gain, gate_up, expert_ids, slot_ids, capacity)
    summed = lax.psum(partial_value, "expert").astype(jnp.bfloat16)
    gathered = lax.all_gather(summed[None], ("dp", "ctx"), axis=0, tiled=True)
    gathered = gathered.reshape(
        dp_count, ctx_count, seq_count, ctx_count, group_count, per_block, col_width
    )
    tokens = jnp.transpose(gathered, (0, 3, 4, 2, 5, 1, 6)).reshape(
        device_count, row_count, model_width
    )
    me = (lax.axis_index("dp") * ctx_count + lax.axis_index("ctx")) * group_count + lax.axis_index(
        "expert"
    )
    mamba_out = lax.dynamic_index_in_dim(tokens, me, axis=0, keepdims=False).reshape(
        seq_count, per_block, model_width
    )
    flat = tokens.reshape(device_count * row_count, model_width).astype(jnp.float32)
    scale = lax.rsqrt(jnp.mean(flat * flat, axis=1, keepdims=True) + 1e-05)
    normed = (flat * scale * moe_gain[None, :]).astype(jnp.bfloat16)
    chosen = routes[..., 0].reshape(device_count, row_count, pick_count)
    placed = routes[..., 1].reshape(device_count, row_count, pick_count)
    target = jnp.arange(device_count)[:, None, None] * capacity + placed
    mine = chosen == lax.axis_index("expert")
    slot_count = device_count * capacity
    hit = mine[..., None] & (target[..., None] == jnp.arange(slot_count))
    selector = jnp.any(hit, axis=2).reshape(device_count * row_count, slot_count)
    dispatched = jnp.einsum(
        "rq,rd->qd", selector.astype(jnp.bfloat16), normed, preferred_element_type=jnp.float32
    ).astype(jnp.bfloat16)
    hidden = expert_ffn(gate_up, dispatched)
    return (mamba_out, hidden[None])


def solution(mesh):
    in_specs = (
        P("dp", "ctx", "expert"),
        P("dp", "ctx", "expert"),
        P("dp", "ctx", None),
        P("dp", "ctx", None),
        P("dp", "ctx", "expert"),
        P("expert"),
        P("expert", "ctx"),
        P(),
        P("expert", None, ("dp", "ctx"), None),
        P("dp", ("ctx", "expert"), None),
        P("dp", ("ctx", "expert"), None),
    )
    out_specs = (P("dp", ("ctx", "expert"), None), P("expert", ("dp", "ctx"), None))
    return jax.shard_map(local, mesh=mesh, in_specs=in_specs, out_specs=out_specs, check_vma=False)
```

profile of v0, /device:TPU:0, one launch (start us, length us, event | category | flops | bytes accessed | tf_op | source)
XLA Modules:
  0.0 197.7 jit_solution(9487829076397545816)
XLA Ops:
  7.2 0.0 all-gather.5.cloned.1.call-start
  7.2 1.7 pad_maximum_fusion
  8.9 0.0 all-gather.5.cloned.1.call-update
  9.0 0.0 all-gather.7.cloned.1.call-start
  9.0 0.7 pad_add_fusion
  9.7 71.7 %all-gather = s32[64,4,2,2]{1,2,0,3:T(2,128)S(1)} all-gather(s32[2,4,2,2]{1,2,0,3:T(2,128)S(1)} %pad_add_fusion), channel_id=2, replica_groups=mesh['dp'=2,'ctx'=4,'expert'=4] {'dp','ctx','expert'}, dimensions={0}, use_global_device_ids=true | all-gather | bytes 4224 | tf_op jit(solution)/shard_map/all_gather | solution.py:105
  81.4 13.3 %all_gather.13 = f32[2,64,32]{2,1,0:T(8,128)S(1)} all-gather(f32[2,16,32]{2,1,0:T(8,128)} %param.15), channel_id=1, replica_groups=mesh['dp'=2,'ctx'=4,'expert'=4] {'ctx'}, dimensions={1}, use_global_device_ids=true | all-gather | bytes 20480 | tf_op jit(solution)/shard_map/all_gather | solution.py:103
  94.8 0.0 all-gather.5.cloned.1.call-done
  94.8 0.9 fusion.37
  95.7 1.2 fusion.42
  96.9 0.1 reduce_window_sum.11
  97.0 0.1 copy.41
  97.1 0.0 copy-start.2
  97.1 1.3 copy.52
  98.4 0.6 copy.53
  99.0 0.0 copy-done.2
  99.0 4.8 %bitcast_add_fusion = f32[2,1,64,32,64]{2,4,3,0,1:T(8,128)} fusion(f32[2,1,64,32,64]{2,4,3,0,1:T(8,128)S(1)} %bitcast.46, bf16[2,64,32,64]{1,3,2,0:T(8,128)(2,1)} %bitcast.49, f32[32]{0:T(128)S(1)} %copy-done.2, f32[2,64,64]{2,1,0:T(8,128)S(1)} %fusion.37, f32[2,64,32]{1,2,0:T(8,128)S(1)} %copy.41, pred[64,64]{1,0:T(8,128)(4,1)S(1)} %iota_compare_fusion.1), kind=kOutput, calls=%fused_computation.11 | convolution fusion | flops 202899456 | bytes 2674816 | tf_op jit(solution)/shard_map/sktuh,skuhp->skthp/dot_general | solution.py:25
  103.8 0.0 copy-start
  103.8 2.3 %copy.54 = f32[2,64,2048]{2,1,0:T(8,128)S(1)} copy(f32[2,64,2048]{1,2,0:T(8,128)} %bitcast.47) | data formatting | bytes 2097152 | tf_op jit(solution)/shard_map/reshape | solution.py:45
  106.1 0.0 copy-done
  106.1 0.0 copy-start.1
  106.1 3.0 %fusion.6 = f32[2,64,1024]{2,1,0:T(8,128)S(1)} fusion(bf16[2048,1024]{1,0:T(8,128)(2,1)} %param.17, f32[2,64,2048]{2,1,0:T(8,128)S(1)} %copy.54, bf16[2,64,4352]{2,1,0:T(8,128)(2,1)S(1)} %copy-done), kind=kOutput, calls=%fused_computation.9 | convolution fusion | flops 538705920 | bytes 6291456 | tf_op jit(solution)/shard_map/stk,kd->std/dot_general | solution.py:113
  109.1 23.6 %all-reduce.1 = bf16[2,64,1024]{2,1,0:T(8,128)(2,1)} all-reduce(f32[2,64,1024]{2,1,0:T(8,128)S(1)} %fusion.6), channel_id=1, replica_groups=mesh['dp'=2,'ctx'=4,'expert'=4] {'expert'}, use_global_device_ids=true, to_apply=%region_1.2 | all-reduce | flops 131072 | bytes 786432 | tf_op jit(solution)/shard_map/psum | solution.py:116
  132.8 0.0 all-gather.7.cloned.1.call-update
  132.8 0.0 copy-done.1
  132.8 0.1 copy.47
  133.0 0.1 copy.48
  133.1 0.1 copy.50
  133.2 0.2 fusion.34
  133.4 26.2 %all-gather.7.cloned.1.call-done = bf16[16,64,1024]{2,1,0:T(8,128)(2,1)} async-done(((bf16[2,64,1024]{2,1,0:T(8,128)(2,1)}), bf16[16,64,1024]{2,1,0:T(8,128)(2,1)}) %all-gather.7.cloned.1.call-update) | async-done | bytes 2097168 | tf_op jit(solution)/shard_map/all_gather | solution.py:117
  159.6 2.7 %reshape.131 = bf16[2,4,2,4,4,4,1024]{6,5,4,3,2,1,0:T(4,128)(2,1)S(1)} reshape(bf16[16,64,1024]{2,1,0:T(8,128)(2,1)} %all-gather.7.cloned.1.call-done) | data formatting | bytes 4194304 | tf_op jit(solution)/shard_map/reshape | solution.py:118
  162.4 2.1 %fusion.3 = f32[2,4,4,2,4]{4,3,2,1,0:T(2,128)S(1)} fusion(bf16[2,4,2,4,4,4,1024]{6,5,4,3,2,1,0:T(4,128)(2,1)S(1)} %reshape.131), kind=kLoop, calls=%fused_computation.6 | loop fusion | flops 3145472 | bytes 2098176 | tf_op jit(solution)/shard_map/reduce_sum | solution.py:131
  164.5 4.2 %copy.61 = bf16[2,4,2,4,4,4,1024]{6,1,5,2,4,3,0:T(4,128)(2,1)} copy(bf16[2,4,2,4,4,4,1024]{6,5,4,3,2,1,0:T(4,128)(2,1)S(1)} %reshape.131) | data formatting | bytes 4194304 | tf_op jit(solution)/shard_map/reshape | solution.py:118
  168.7 4.5 %reshape.132 = bf16[32,8,4096]{2,1,0:T(8,128)(2,1)} reshape(bf16[2,4,4,2,4,4,1024]{6,5,4,3,2,1,0:T(4,128)(2,1)} %bitcast.45) | data formatting | bytes 4194304 | tf_op jit(solution)/shard_map/reshape | solution.py:121
  173.2 0.8 constant_dynamic-slice_fusion
  174.1 0.7 reshape.133
  174.7 2.6 %fusion.5 = bf16[2,4,4,2,4,4,1024]{6,5,4,3,2,1,0:T(4,128)(2,1)S(1)} fusion(f32[4,1024]{1,0:T(4,128)S(1)} %mul.97, f32[2,4,4,2,4]{4,3,2,1,0:T(2,128)S(1)} %add_rsqrt_fusion, bf16[2,4,2,4,4,4,1024]{6,5,4,3,2,1,0:T(4,128)(2,1)S(1)} %reshape.131), kind=kLoop, calls=%fused_computation.8 | loop fusion | flops 4194304 | bytes 4211712 | tf_op jit(solution)/shard_map/convert_element_type | solution.py:132
  177.4 0.9 copy.55
  178.2 9.9 %fusion.16 = f32[2,896,256]{1,2,0:T(8,128)} fusion(bf16[1,2,896,4096]{3,2,1,0:T(8,128)(2,1)} %param.19, bf16[256,4096]{1,0:T(8,128)(2,1)S(1)} %bitcast.48, pred[32,8,256]{2,1,0:T(8,128)(4,1)S(1)} %fusion.34), kind=kOutput, calls=%fused_computation.19 | convolution fusion | flops 4296015872 | bytes 18677760 | tf_op jit(solution)/shard_map/gfd,qd->gfq/dot_general | solution.py:49
  188.2 1.7 fusion.29
  189.9 1.0 copy.51
  (7 shorter events, 0.1 us)
Async XLA Ops:
  7.2 87.6 %all-gather.5.cloned.1.call-start = ((), (), s32[]{:S(2)}) async-start(), calls=%async_computation | async-start | bytes 1392640 | tf_op jit(solution)/shard_map/all_gather | solution.py:102
  9.0 150.7 %all-gather.7.cloned.1.call-start = ((), (), s32[]{:S(2)}) async-start(), calls=%async_computation.1 | async-start | bytes 2359296 | tf_op jit(solution)/shard_map/all_gather | solution.py:117
  97.1 1.9 copy-start.2
  103.8 2.3 %copy-start = (bf16[2,64,4352]{2,1,0:T(8,128)(2,1)S(1)}, bf16[2,64,4352]{2,1,0:T(8,128)(2,1)}, u32[]{:S(2)}) copy-start(bf16[2,64,4352]{2,1,0:T(8,128)(2,1)} %all-gather.5.cloned.1.call-done) | copy-start | bytes 3342340
  106.1 26.7 %copy-start.1 = (f32[4096]{0:T(1024)S(1)}, f32[4096]{0:T(1024)}, u32[]{:S(2)}) copy-start(f32[4096]{0:T(1024)} %param.18) | copy-start | bytes 49156
Sparse Core Ops, SparseCore 0:
  10.1 32.3 all-gather.4
  132.9 26.6 all-gather.6
where the time goes:
time: 198 us
  blocking collectives  109 us (55%)
  waiting for transfers between devices  26.3 us (13%)
  local copies, waits for them, and re-layouts  19.4 us (10%)
  matrix products  18.6 us (9%)
  between operations  14.2 us (7%)
  other arithmetic  10.5 us (5%)
    all_gather x1, blocking collectives, local(): routes = lax.all_gather(route[None], ALL_AXES, axis=0, tiled=True)  71.7 us
    all_gather x1, waiting for transfers between devices, local(): gathered = lax.all_gather(summed[None], ('dp', 'ctx'), axis=0, tiled=True)  26.2 us
    psum x1, blocking collectives, local(): summed = lax.psum(partial_value, 'expert').astype(jnp.bfloat16)  23.6 us
    all_gather x1, blocking collectives, local(): decay_all = lax.all_gather(decay_log, 'ctx', axis=1, tiled=True)  13.3 us
    dot_general x1, matrix products, expert_ffn(): jnp.einsum('gfd,qd->gfq', gate_up[0], slot_rows, preferred_element_type=j...  9.91 us
    reshape x2, local copies, waits for them, and re-layouts, local(): gathered.reshape(dp_count, ctx_count, seq_count, ctx_count, group_count,...  6.91 us
    dot_general x1, matrix products, mixer(): ssd = jnp.einsum('sktuh,skuhp->skthp', kernel, x_float, precision=highest)  4.79 us
    reshape x1, local copies, waits for them, and re-layouts, local(): jnp.transpose(gathered, (0, 3, 4, 2, 5, 1, 6))  4.48 us
  transfers between devices with their start and end apart: 2, of which 1 were waited for; matrix products, arithmetic and copies ran while one was open for 1% of the time, Pallas kernels for 0%

commit v1 on v0

--- a/solution.py
+++ b/solution.py
@@ -113,7 +113,7 @@
     partial_value = jnp.einsum("stk,kd->std", gated, out_weight, preferred_element_type=jnp.float32)
     if device_count * row_count * model_width * 2 > 8 << 20:
         return dispatch_routed(partial_value, moe_gain, gate_up, expert_ids, slot_ids, capacity)
-    summed = lax.psum(partial_value, "expert").astype(jnp.bfloat16)
+    summed = jnp.sum(lax.all_gather(partial_value, "expert"), axis=0).astype(jnp.bfloat16)
     gathered = lax.all_gather(summed[None], ("dp", "ctx"), axis=0, tiled=True)
     gathered = gathered.reshape(
         dp_count, ctx_count, seq_count, ctx_count, group_count, per_block, col_width

time: 198 us -> 213 us (1.076)
  waiting for transfers between devices: 26.3 us -> 60.2 us
  blocking collectives: 109 us -> 85 us
    all_gather x0 -> x1, waiting for transfers between devices: none -> 31.4 us  [local(): lax.all_gather(partial_value, 'expert')]
    psum x1 -> x0, blocking collectives: 23.6 us -> none  [local(): summed = lax.psum(partial_value, 'expert').astype(jnp.bfloat16)]
    reshape x2 -> x1, local copies, waits for them, and re-layouts: 6.91 us -> 2.73 us  [local(): gathered.reshape(dp_count, ctx_count, seq_count, ctx_count, group_count,...]
    transpose x0 -> x1, local copies, waits for them, and re-layouts: none -> 4.17 us  [local(): jnp.transpose(gathered, (0, 3, 4, 2, 5, 1, 6))]
    convert_element_type x0 -> x1, local copies, waits for them, and re-layouts: none -> 2.82 us  [local(): normed = (flat * scale * moe_gain[None, :]).astype(jnp.bfloat16)]
    reduce_sum x0 -> x1, other arithmetic: none -> 2.52 us  [local(): jnp.sum(lax.all_gather(partial_value, 'expert'), axis=0)]
    all_gather x1, waiting for transfers between devices: 26.2 us -> 28.7 us  [local(): gathered = lax.all_gather(summed[None], ('dp', 'ctx'), axis=0, tiled=True)]
  transfers between devices with their start and end apart: 2 -> 3, of which waited for: 1 -> 2; matrix products, arithmetic and copies ran while one was open for 1% -> 1% of each run, Pallas kernels for 0% -> 0%
where the time goes in v1:
time: 213 us; the launch traced here: 212 us
  blocking collectives  85 us (40%)
  waiting for transfers between devices  60.2 us (28%)
  local copies, waits for them, and re-layouts  21.4 us (10%)
  matrix products  19.9 us (9%)
  between operations  13.9 us (7%)
  other arithmetic  11.3 us (5%)
    all_gather x1, blocking collectives, local(): routes = lax.all_gather(route[None], ALL_AXES, axis=0, tiled=True)  71.7 us
    all_gather x1, waiting for transfers between devices, local(): lax.all_gather(partial_value, 'expert')  31.4 us
    all_gather x1, waiting for transfers between devices, local(): gathered = lax.all_gather(summed[None], ('dp', 'ctx'), axis=0, tiled=True)  28.7 us
    all_gather x1, blocking collectives, local(): decay_all = lax.all_gather(decay_log, 'ctx', axis=1, tiled=True)  13.3 us
    dot_general x1, matrix products, expert_ffn(): jnp.einsum('gfd,qd->gfq', gate_up[0], slot_rows, preferred_element_type=j...  10.5 us
    dot_general x1, matrix products, mixer(): ssd = jnp.einsum('sktuh,skuhp->skthp', kernel, x_float, precision=highest)  4.78 us
  transfers between devices with their start and end apart: 3, of which 2 were waited for; matrix products, arithmetic and copies ran while one was open for 1% of the time, Pallas kernels for 0%

profile of v1, /device:TPU:0, one launch (start us, length us, event | category | flops | bytes accessed | tf_op | source)
XLA Modules:
  0.0 212.2 jit_solution(2830134750785641175)
XLA Ops:
  7.2 0.0 all-gather.7.cloned.1.call-start
  7.2 1.7 pad_maximum_fusion
  8.9 0.0 all-gather.7.cloned.1.call-update
  9.0 0.0 all-gather.9.cloned.1.call-start
  9.0 0.7 pad_add_fusion
  9.7 71.7 %all-gather = s32[64,4,2,2]{1,2,0,3:T(2,128)S(1)} all-gather(s32[2,4,2,2]{1,2,0,3:T(2,128)S(1)} %pad_add_fusion), channel_id=2, replica_groups=mesh['dp'=2,'ctx'=4,'expert'=4] {'dp','ctx','expert'}, dimensions={0}, use_global_device_ids=true | all-gather | bytes 4224 | tf_op jit(solution)/shard_map/all_gather | solution.py:105
  81.4 13.3 %all_gather.19 = f32[2,64,32]{2,1,0:T(8,128)S(1)} all-gather(f32[2,16,32]{2,1,0:T(8,128)} %param.15), channel_id=1, replica_groups=mesh['dp'=2,'ctx'=4,'expert'=4] {'ctx'}, dimensions={1}, use_global_device_ids=true | all-gather | bytes 20480 | tf_op jit(solution)/shard_map/all_gather | solution.py:103
  94.8 0.0 all-gather.7.cloned.1.call-done
  94.8 0.9 fusion.37
  95.7 1.2 fusion.42
  96.9 0.1 reduce_window_sum.11
  97.0 0.1 copy.53
  97.1 0.0 copy-start.2
  97.1 1.3 copy.65
  98.4 0.6 copy.66
  99.0 0.0 copy-done.2
  99.0 4.8 %bitcast_add_fusion = f32[2,1,64,32,64]{2,4,3,0,1:T(8,128)} fusion(f32[2,1,64,32,64]{2,4,3,0,1:T(8,128)S(1)} %bitcast.44, bf16[2,64,32,64]{1,3,2,0:T(8,128)(2,1)} %bitcast.47, f32[32]{0:T(128)S(1)} %copy-done.2, f32[2,64,64]{2,1,0:T(8,128)S(1)} %fusion.37, f32[2,64,32]{1,2,0:T(8,128)S(1)} %copy.53, pred[64,64]{1,0:T(8,128)(4,1)S(1)} %iota_compare_fusion.1), kind=kOutput, calls=%fused_computation.11 | convolution fusion | flops 202899456 | bytes 2674816 | tf_op jit(solution)/shard_map/sktuh,skuhp->skthp/dot_general | solution.py:25
  103.8 0.0 copy-start
  103.8 2.3 %copy.67 = f32[2,64,2048]{2,1,0:T(8,128)S(1)} copy(f32[2,64,2048]{1,2,0:T(8,128)} %bitcast.45) | data formatting | bytes 2097152 | tf_op jit(solution)/shard_map/reshape | solution.py:45
  106.1 0.0 copy-done
  106.1 3.8 %fusion.6 = f32[2,64,1024]{2,1,0:T(8,128)} fusion(bf16[2048,1024]{1,0:T(8,128)(2,1)} %param.17, f32[2,64,2048]{2,1,0:T(8,128)S(1)} %copy.67, bf16[2,64,4352]{2,1,0:T(8,128)(2,1)S(1)} %copy-done), kind=kOutput, calls=%fused_computation.9 | convolution fusion | flops 538705920 | bytes 6291456 | tf_op jit(solution)/shard_map/stk,kd->std/dot_general | solution.py:113
  109.9 0.0 copy-start.1
  109.9 0.0 all-gather.9.cloned.1.call-update
  109.9 0.2 all-gather.11.cloned.1.call-start
  110.1 31.4 %all-gather.9.cloned.1.call-done = f32[8,64,1024]{2,1,0:T(8,128)} async-done(((f32[2,64,1024]{2,1,0:T(8,128)}), f32[8,64,1024]{2,1,0:T(8,128)}) %all-gather.9.cloned.1.call-update) | async-done | bytes 2097168 | tf_op jit(solution)/shard_map/all_gather | solution.py:116
  141.6 2.5 %reduce_sum.18 = bf16[2,64,1024]{2,1,0:T(8,128)(2,1)} reduce(f32[4,2,64,1024]{3,2,1,0:T(8,128)} %bitcast.43, f32[]{:T(128)} %constant.14.clone.1), dimensions={0}, to_apply=%region_1.2 | reduce | flops 393216 | bytes 2359300 | tf_op jit(solution)/shard_map/reduce_sum | solution.py:116
  144.1 0.0 all-gather.11.cloned.1.call-update
  144.1 0.0 copy-done.1
  144.2 0.1 copy.59
  144.3 0.1 copy.60
  144.4 0.1 copy.62
  144.5 0.2 fusion.34
  144.8 28.7 %all-gather.11.cloned.1.call-done = bf16[16,64,1024]{2,1,0:T(8,128)(2,1)} async-done(((bf16[2,64,1024]{2,1,0:T(8,128)(2,1)}), bf16[16,64,1024]{2,1,0:T(8,128)(2,1)}) %all-gather.11.cloned.1.call-update) | async-done | bytes 2097168 | tf_op jit(solution)/shard_map/all_gather | solution.py:117
  173.4 2.7 %reshape.139 = bf16[2,4,2,4,4,4,1024]{6,5,4,3,2,1,0:T(4,128)(2,1)S(1)} reshape(bf16[16,64,1024]{2,1,0:T(8,128)(2,1)} %all-gather.11.cloned.1.call-done) | data formatting | bytes 4194304 | tf_op jit(solution)/shard_map/reshape | solution.py:118
  176.2 1.2 fusion.3
  177.4 1.9 fusion.5
  179.3 2.8 %copy.63 = bf16[2,4,4,2,4,4,1024]{6,5,4,3,2,1,0:T(4,128)(2,1)S(1)} copy(bf16[2,4,4,2,4,4,1024]{6,4,2,1,3,5,0:T(4,128)(2,1)S(1)} %fusion.5) | data formatting | bytes 4194304 | tf_op jit(solution)/shard_map/convert_element_type | solution.py:132
  182.1 2.2 %copy.68 = bf16[32,8,4,1024]{3,1,2,0:T(8,128)(2,1)} copy(bf16[32,8,4,1024]{3,2,1,0:T(4,128)(2,1)S(1)} %bitcast.42) | data formatting | bytes 4194304
  184.3 10.5 %fusion.16 = f32[2,896,256]{1,2,0:T(8,128)} fusion(bf16[1,2,896,4096]{3,2,1,0:T(8,128)(2,1)} %param.19, bf16[256,4096]{1,0:T(8,128)(2,1)} %bitcast.46, pred[32,8,256]{2,1,0:T(8,128)(4,1)S(1)} %fusion.34), kind=kOutput, calls=%fused_computation.18 | convolution fusion | flops 4296015872 | bytes 18677760 | tf_op jit(solution)/shard_map/gfd,qd->gfq/dot_general | solution.py:49
  194.8 1.7 fusion.29
  196.5 1.0 copy.64
  197.5 4.2 %copy.58 = bf16[2,4,4,2,4,4,1024]{6,5,4,3,2,1,0:T(4,128)(2,1)} copy(bf16[2,4,4,2,4,4,1024]{6,4,2,1,3,5,0:T(4,128)(2,1)S(1)} %bitcast.41) | data formatting | bytes 4194304 | tf_op jit(solution)/shard_map/transpose | solution.py:121
  201.7 3.3 %reshape.140 = bf16[32,8,4096]{2,1,0:T(8,128)(2,1)S(1)} reshape(bf16[2,4,4,2,4,4,1024]{6,5,4,3,2,1,0:T(4,128)(2,1)} %copy.58) | data formatting | bytes 4194304 | tf_op jit(solution)/shard_map/reshape | solution.py:121
  205.0 0.7 reshape.141
  (8 shorter events, 0.1 us)
Async XLA Ops:
  7.2 87.6 %all-gather.7.cloned.1.call-start = ((), (), s32[]{:S(2)}) async-start(), calls=%async_computation | async-start | bytes 1392640 | tf_op jit(solution)/shard_map/all_gather | solution.py:102
  9.0 132.6 %all-gather.9.cloned.1.call-start = ((), (), s32[]{:S(2)}) async-start(), calls=%async_computation.1 | async-start | bytes 2621440 | tf_op jit(solution)/shard_map/all_gather | solution.py:116
  97.1 1.9 copy-start.2
  103.8 2.3 %copy-start = (bf16[2,64,4352]{2,1,0:T(8,128)(2,1)S(1)}, bf16[2,64,4352]{2,1,0:T(8,128)(2,1)}, u32[]{:S(2)}) copy-start(bf16[2,64,4352]{2,1,0:T(8,128)(2,1)} %all-gather.7.cloned.1.call-done) | copy-start | bytes 3342340
  109.9 34.3 %copy-start.1 = (f32[4096]{0:T(1024)S(1)}, f32[4096]{0:T(1024)}, u32[]{:S(2)}) copy-start(f32[4096]{0:T(1024)} %param.18) | copy-start | bytes 49156
  109.9 63.5 %all-gather.11.cloned.1.call-start = ((), (), s32[]{:S(2)}) async-start(), calls=%async_computation.2 | async-start | bytes 2359296 | tf_op jit(solution)/shard_map/all_gather | solution.py:117
Sparse Core Ops, SparseCore 0:
  10.1 32.3 all-gather.6
  110.0 31.5 all-gather.8
  144.2 29.1 all-gather.10
